TPU v7x, 256 devices: a whole 4x4x8 slice. The times are simulated.
256 devices in a mesh: link: 64 (over x, z, core), col: 4 (over y).
Axes of the slice: x: 4, y: 4, z: 8, core: 2. Of those that a mesh axis runs over, the one named last changes fastest.
Arguments:
- values: bfloat16 [1024, 16, 128], P('link'), may hold values from -6 to 6
- tiles: int32 [1024, 16], P('link'), may hold values from 0 to 127, all different within a row
- barrier: float32 [1024], P('link'), may hold values from 0.5 to 2
- slack: float32 [16384], replicated, may hold values from 0.5 to 2
- order: int32 [128], replicated, may hold values from 0 to 127, each once
Outputs:
- factored: float32 [16384, 16384], P('link', 'col')
Inputs may be any that keep to these rules, and one draw needn't show every extreme that they name: `tiles`: each commodity's 16 tile numbers are distinct, and every tile is named by some commodity. `order`: each tile number appears once.
All inputs are finite; a program needn't handle non-finite values.
Results may differ from a plain program's by a relative error of at most 0.0038.
Values may be sent and summed in bfloat16 or wider, within the bound.
No kernel may reach another device: no remote copies, remote signals or barrier semaphores. Data moves between devices by JAX's collectives and lax.ppermute only.
A program may use at most 64 MiB of HBM per device.

v0:
```python
import jax
import jax.numpy as jnp
from jax import lax
from jax.sharding import PartitionSpec as P

PANEL = 128


def spread(value, axis, source):
    kept = jnp.where(lax.axis_index(axis) == source, value, 0).astype(value.dtype)
    return lax.psum(kept, axis)


def densify(tile_vals, tile_ids, targets):
    onehot = (tile_ids[:, :, None] == targets[None, None, :]).astype(jnp.bfloat16)
    dense_out = jnp.einsum("kjp,kju->kpu", onehot, tile_vals, preferred_element_type=jnp.float32)
    dense_out = dense_out.astype(jnp.bfloat16)
    return dense_out.reshape(tile_vals.shape[0], targets.shape[0] * tile_vals.shape[2])


def contract_rows(left_side, right_side):
    return lax.dot_general(
        left_side, right_side, (((0,), (0,)), ((), ())), preferred_element_type=jnp.float32
    )


def local(values, tiles, barrier, slack, order):
    link_devs = lax.axis_size("link")
    col_devs = lax.axis_size("col")
    link_idx = lax.axis_index("link")
    col_idx = lax.axis_index("col")
    link_count = slack.shape[0]
    rows_dev = link_count // link_devs
    cols_dev = link_count // col_devs
    tile_len = values.shape[2]
    ntiles = order.shape[0]
    factor = link_count / (values.shape[0] * link_devs * values.shape[1] * tile_len)
    scaled = (jnp.sqrt(barrier * factor)[:, None, None] * values.astype(jnp.float32)).astype(
        jnp.bfloat16
    )
    own_dense = densify(scaled, tiles, order)
    link_rows = lax.all_to_all(own_dense, "link", split_axis=1, concat_axis=0, tiled=True)
    col_slab = lax.dynamic_slice_in_dim(own_dense, col_idx * cols_dev, cols_dev, 1)
    normal = contract_rows(link_rows, lax.all_gather(col_slab, "link", axis=0, tiled=True))
    rows_g = link_idx * rows_dev + jnp.arange(rows_dev)
    cols_g = col_idx * cols_dev + jnp.arange(cols_dev)
    perm_hot = (order[:, None] == jnp.arange(ntiles)[None, :]).astype(jnp.float32)
    slack_ord = jnp.dot(
        perm_hot, slack.reshape(ntiles, tile_len), precision=lax.Precision.HIGHEST
    ).reshape(link_count)
    slack_rows = lax.dynamic_slice_in_dim(slack_ord, link_idx * rows_dev, rows_dev)
    matrix = normal + jnp.where(
        rows_g[:, None] == cols_g[None, :], slack_rows[:, None], jnp.float32(0.0)
    )
    panels = []
    for panel_no in range(2):
        first_col = panel_no * PANEL
        diag_block = matrix[first_col : first_col + PANEL, first_col : first_col + PANEL]
        factor_local = jnp.linalg.cholesky(diag_block)
        lower_fac = spread(factor_local, "link", 0)
        solved = jax.scipy.linalg.solve_triangular(
            lower_fac, matrix[:, first_col : first_col + PANEL].T, lower=True
        ).T
        picker = ((rows_g - first_col)[:, None] == jnp.arange(PANEL)[None, :]).astype(jnp.float32)
        diag_rows = jnp.dot(picker, lower_fac, precision=lax.Precision.HIGHEST)
        column = jnp.where(
            rows_g[:, None] < first_col,
            jnp.float32(0.0),
            jnp.where(rows_g[:, None] < first_col + PANEL, diag_rows, solved),
        )
        across = spread(column.astype(jnp.bfloat16), "col", 0)
        everyone = lax.all_gather(across, "link", axis=0, tiled=True)
        col_part = lax.dynamic_slice_in_dim(everyone, col_idx * cols_dev, cols_dev, 0)
        matrix = matrix - lax.dot_general(
            across, col_part, (((1,), (1,)), ((), ())), preferred_element_type=jnp.float32
        )
        panels.append(column)
    panel_block = jnp.concatenate(panels, 1)
    padded = jnp.pad(panel_block, ((0, 0), (0, cols_dev - 2 * PANEL)))
    return jnp.where(
        cols_g[None, :] < 2 * PANEL,
        padded,
        jnp.where(rows_g[:, None] < 2 * PANEL, jnp.float32(0.0), matrix),
    )


def solution(mesh):
    in_specs = (P("link", None, None), P("link", None), P("link"), P(), P())
    out_specs = P("link", "col")
    return jax.shard_map(local, mesh=mesh, in_specs=in_specs, out_specs=out_specs, check_vma=False)
```

profile of v0, /device:TPU:1, one launch (start us, length us, event | category | flops | bytes accessed | tf_op | source)
XLA Modules:
  0.0 768.8 jit_solution(11925922518593524493)
XLA Ops:
  6.5 0.0 copy-start
  6.5 0.0 copy-start.3
  6.5 0.0 all-gather.4.cloned.1.call-start
  6.5 0.7 multiply_sqrt_fusion
  7.2 1.4 convolution_convert_fusion
  8.6 0.3 copy.24
  9.0 0.7 constant_dynamic-slice_fusion
  9.7 0.0 all-gather.4.cloned.1.call-update
  9.7 0.2 all_to_all.14
  9.9 1.1 copy.12
  10.9 13.0 %all-to-all-start = ((bf16[16,64,256]{2,0,1:T(8,128)(2,1)}), bf16[16,64,256]{2,0,1:T(8,128)(2,1)S(1)}, u32[]{:S(2)}, u32[]{:S(2)}) async-start(bf16[16,64,256]{2,0,1:T(8,128)(2,1)} %copy.12), calls=%async_computation | async-start | bytes 1048576 | tf_op jit(solution)/shard_map/all_to_all | solution.py:42
  23.9 0.0 all-reduce.6.cloned.1.call-start
  24.0 0.0 copy-done
  24.0 0.0 copy-done.3
  24.0 0.2 convolution_bitcast_fusion
  24.2 0.1 dynamic_slice.13
  24.3 19.3 %all-to-all-done = bf16[16,64,256]{2,0,1:T(8,128)(2,1)S(1)} async-done(((bf16[16,64,256]{2,0,1:T(8,128)(2,1)}), bf16[16,64,256]{2,0,1:T(8,128)(2,1)S(1)}, u32[]{:S(2)}, u32[]{:S(2)}) %all-to-all-start) | async-done | bytes 524320 | tf_op jit(solution)/shard_map/all_to_all | solution.py:42
  43.6 54.6 %all-gather.4.cloned.1.call-done = bf16[1024,4096]{1,0:T(8,128)(2,1)} async-done(((bf16[16,4096]{1,0:T(8,128)(2,1)}), bf16[1024,4096]{1,0:T(8,128)(2,1)}) %all-gather.4.cloned.1.call-update) | async-done | bytes 8388624 | tf_op jit(solution)/shard_map/all_gather | solution.py:44
  98.2 6.6 convolution_add_fusion
  104.8 0.0 copy-start.1
  104.8 2.0 copy-done.1
  106.8 0.1 copy.14
  106.9 0.9 fusion.14
  107.8 11.7 %cholesky.44 = f32[128,128]{1,0:T(8,128)S(1)} custom-call(f32[128,128]{1,0:T(8,128)S(1)} %fusion.14), custom_call_target="Cholesky" | custom-call | tf_op jit(solution)/shard_map/jit(cholesky)/cholesky | solution.py:59
  119.5 0.7 compare_reduce_fusion.1
  120.2 1.3 select_select_fusion.1
  121.5 0.0 all-reduce.6.cloned.1.call-update
  121.5 0.0 all-reduce.8.cloned.1.call-start
  121.6 167.5 %all-reduce.6.cloned.1.call-done = f32[128,128]{1,0:T(8,128)} async-done(((f32[128,128]{1,0:T(8,128)}), f32[128,128]{1,0:T(8,128)}) %all-reduce.6.cloned.1.call-update) | async-done | bytes 65552 | tf_op jit(solution)/shard_map/psum | solution.py:11
  289.1 0.8 select_bitcast_fusion.1
  289.9 9.8 %custom-call.6 = f32[1,128,128]{1,2,0:T(8,128)S(1)} custom-call(f32[1,128,128]{2,1,0:T(8,128)S(1)} %select_bitcast_fusion.1), custom_call_target="InvertDiagBlocksLowerTriangular" | custom-call | tf_op jit(solution)/shard_map/jit(_solve_triangular)/triangular_solve | solution.py:61
  299.7 1.1 fusion.8
  300.9 1.9 convert_select_fusion.1
  302.7 0.0 all-reduce.8.cloned.1.call-update
  302.8 0.0 all-gather.6.cloned.1.call-start
  302.8 41.2 %all-reduce.8.cloned.1.call-done = bf16[256,128]{0,1:T(8,128)(2,1)} async-done(((bf16[256,128]{0,1:T(8,128)(2,1)}), bf16[256,128]{0,1:T(8,128)(2,1)}) %all-reduce.8.cloned.1.call-update) | async-done | bytes 65552 | tf_op jit(solution)/shard_map/psum | solution.py:11
  344.0 0.0 all-gather.6.cloned.1.call-update
  344.0 0.2 all-reduce.10.cloned.1.call-start
  344.3 81.0 %all-gather.6.cloned.1.call-done = bf16[16384,128]{0,1:T(8,128)(2,1)} async-done(((bf16[256,128]{0,1:T(8,128)(2,1)}), bf16[16384,128]{0,1:T(8,128)(2,1)}) %all-gather.6.cloned.1.call-update) | async-done | bytes 4194320 | tf_op jit(solution)/shard_map/all_gather | solution.py:72
  425.2 3.3 convolution_subtract_fusion.1
  428.5 0.0 copy-start.2
  428.6 2.0 copy-done.2
  430.6 0.1 copy.16
  430.7 0.9 fusion.12
  431.5 11.7 %cholesky.55 = f32[128,128]{1,0:T(8,128)S(1)} custom-call(f32[128,128]{1,0:T(8,128)S(1)} %fusion.12), custom_call_target="Cholesky" | custom-call | tf_op jit(solution)/shard_map/jit(cholesky)/cholesky | solution.py:59
  443.3 0.7 compare_reduce_fusion
  443.9 1.3 select_select_fusion
  445.2 0.0 all-reduce.10.cloned.1.call-update
  445.2 0.0 all-reduce.12.cloned.1.call-start
  445.3 170.2 %all-reduce.10.cloned.1.call-done = f32[128,128]{1,0:T(8,128)} async-done(((f32[128,128]{1,0:T(8,128)}), f32[128,128]{1,0:T(8,128)}) %all-reduce.10.cloned.1.call-update) | async-done | bytes 65552 | tf_op jit(solution)/shard_map/psum | solution.py:11
  615.4 0.8 select_bitcast_fusion
  616.3 9.8 %custom-call.7 = f32[1,128,128]{1,2,0:T(8,128)S(1)} custom-call(f32[1,128,128]{2,1,0:T(8,128)S(1)} %select_bitcast_fusion), custom_call_target="InvertDiagBlocksLowerTriangular" | custom-call | tf_op jit(solution)/shard_map/jit(_solve_triangular)/triangular_solve | solution.py:61
  626.1 1.1 fusion.9
  627.3 1.9 convert_select_fusion
  629.1 0.0 all-reduce.12.cloned.1.call-update
  629.1 0.0 all-gather.8.cloned.1.call-start
  629.2 41.2 %all-reduce.12.cloned.1.call-done = bf16[256,128]{0,1:T(8,128)(2,1)} async-done(((bf16[256,128]{0,1:T(8,128)(2,1)}), bf16[256,128]{0,1:T(8,128)(2,1)}) %all-reduce.12.cloned.1.call-update) | async-done | bytes 65552 | tf_op jit(solution)/shard_map/psum | solution.py:11
  670.4 0.0 all-gather.8.cloned.1.call-update
  670.4 81.4 %all-gather.8.cloned.1.call-done = bf16[16384,128]{0,1:T(8,128)(2,1)} async-done(((bf16[256,128]{0,1:T(8,128)(2,1)}), bf16[16384,128]{0,1:T(8,128)(2,1)}) %all-gather.8.cloned.1.call-update) | async-done | bytes 4194320 | tf_op jit(solution)/shard_map/all_gather | solution.py:72
  751.8 4.6 fusion.1
  756.3 5.6 copy.18
  (10 shorter events, 0.1 us)
Async XLA Ops:
  6.5 17.5 %copy-start = (f32[16384]{0:T(1024)S(1)}, f32[16384]{0:T(1024)}, u32[]{:S(2)}) copy-start(f32[16384]{0:T(1024)} %param.11) | copy-start | bytes 196612
  6.5 17.5 %copy-start.3 = (s32[128]{0:T(128)S(1)}, s32[128]{0:T(128)}, u32[]{:S(2)}) copy-start(s32[128]{0:T(128)} %param.12) | copy-start | bytes 1540
  6.5 91.6 %all-gather.4.cloned.1.call-start = ((), (), s32[]{:S(2)}) async-start(), calls=%async_computation.1 | async-start | bytes 8519680 | tf_op jit(solution)/shard_map/all_gather | solution.py:44
  10.9 32.7 %all-to-all-start = ((bf16[16,64,256]{2,0,1:T(8,128)(2,1)}), bf16[16,64,256]{2,0,1:T(8,128)(2,1)S(1)}, u32[]{:S(2)}, u32[]{:S(2)}) async-start(bf16[16,64,256]{2,0,1:T(8,128)(2,1)} %copy.12), calls=%async_computation | async-start | bytes 1048576 | tf_op jit(solution)/shard_map/all_to_all | solution.py:42
  23.9 265.1 %all-reduce.6.cloned.1.call-start = ((), (), s32[]{:S(2)}) async-start(), calls=%async_computation.2 | async-start | bytes 131072 | tf_op jit(solution)/shard_map/psum | solution.py:11
  104.8 2.0 copy-start.1
  121.5 222.5 %all-reduce.8.cloned.1.call-start = ((), (), s32[]{:S(2)}) async-start(), calls=%async_computation.3 | async-start | bytes 131072 | tf_op jit(solution)/shard_map/psum | solution.py:11
  302.8 122.5 %all-gather.6.cloned.1.call-start = ((), (), s32[]{:S(2)}) async-start(), calls=%async_computation.4 | async-start | bytes 4259840 | tf_op jit(solution)/shard_map/all_gather | solution.py:72
  344.0 271.4 %all-reduce.10.cloned.1.call-start = ((), (), s32[]{:S(2)}) async-start(), calls=%async_computation.5 | async-start | bytes 131072 | tf_op jit(solution)/shard_map/psum | solution.py:11
  428.5 2.0 copy-start.2
  445.2 225.1 %all-reduce.12.cloned.1.call-start = ((), (), s32[]{:S(2)}) async-start(), calls=%async_computation.6 | async-start | bytes 131072 | tf_op jit(solution)/shard_map/psum | solution.py:11
  629.1 122.6 %all-gather.8.cloned.1.call-start = ((), (), s32[]{:S(2)}) async-start(), calls=%async_computation.7 | async-start | bytes 4259840 | tf_op jit(solution)/shard_map/all_gather | solution.py:72
Sparse Core Ops, SparseCore 0:
  10.1 88.0 all-gather.3
  121.6 167.4 all-reduce.5
  302.9 41.0 all-reduce.7
  346.4 78.8 all-gather.5
  445.3 170.0 all-reduce.9
  629.3 41.0 all-reduce.11
  672.9 78.8 all-gather.7
where the time goes:
time: 769 us
  waiting for transfers between devices  656 us (85%)
  other arithmetic  51.1 us (7%)
  matrix products  22.1 us (3%)
  between operations  13.7 us (2%)
  starting transfers between devices  13.4 us (2%)
  local copies, waits for them, and re-layouts  12.1 us (2%)
    psum x4, waiting for transfers between devices, spread(): return lax.psum(kept, axis)  420 us
    all_gather x2, waiting for transfers between devices, local(): everyone = lax.all_gather(across, 'link', axis=0, tiled=True)  162 us
    all_gather x1, waiting for transfers between devices, local(): lax.all_gather(col_slab, 'link', axis=0, tiled=True)  54.6 us
    another operation x6, other arithmetic, local(): factor_local = jnp.linalg.cholesky(diag_block)  24.8 us
    another operation x4, other arithmetic, local(): jax.scipy.linalg.solve_triangular(lower_fac, matrix[:, first_col:first_co...  21.3 us
    all_to_all x1, waiting for transfers between devices, local(): lax.all_to_all(own_dense, 'link', split_axis=1, concat_axis=0, tiled=True)  19.3 us
  transfers between devices with their start and end apart: 8, of which 8 were waited for; matrix products, arithmetic and copies ran while one was open for 0% of the time, Pallas kernels for 0%

commit v1 on v0

--- a/solution.py
+++ b/solution.py
@@ -8,7 +8,7 @@
 
 def spread(value, axis, source):
     kept = jnp.where(lax.axis_index(axis) == source, value, 0).astype(value.dtype)
-    return lax.psum(kept, axis)
+    return jnp.sum(lax.all_gather(kept, axis), axis=0)
 
 
 def densify(tile_vals, tile_ids, targets):

time: 769 us -> 514 us (0.67)
  waiting for transfers between devices: 656 us -> 379 us
  blocking collectives: 0 us -> 20.7 us
    psum x4 -> x0, waiting for transfers between devices: 420 us -> none  [spread(): return lax.psum(kept, axis)]
    all_gather x0 -> x2, waiting for transfers between devices: none -> 154 us  [spread(): return jnp.sum(lax.all_gather(kept, axis), axis=0)]
    all_gather x0 -> x2, blocking collectives: none -> 20.7 us  [spread(): return jnp.sum(lax.all_gather(kept, axis), axis=0)]
    all_gather x2, waiting for transfers between devices: 162 us -> 150 us  [local(): everyone = lax.all_gather(across, 'link', axis=0, tiled=True)]
  transfers between devices with their start and end apart: 8 -> 6, of which waited for: 8 -> 6; matrix products, arithmetic and copies ran while one was open for 0% -> 0% of each run, Pallas kernels for 0% -> 0%
where the time goes in v1:
time: 514 us
  waiting for transfers between devices  379 us (74%)
  other arithmetic  56 us (11%)
  blocking collectives  20.7 us (4%)
  matrix products  19.1 us (4%)
  between operations  13.4 us (3%)
  starting transfers between devices  13.3 us (3%)
  local copies, waits for them, and re-layouts  12.5 us (2%)
    all_gather x2, waiting for transfers between devices, spread(): return jnp.sum(lax.all_gather(kept, axis), axis=0)  154 us
    all_gather x2, waiting for transfers between devices, local(): everyone = lax.all_gather(across, 'link', axis=0, tiled=True)  150 us
    all_gather x1, waiting for transfers between devices, local(): lax.all_gather(col_slab, 'link', axis=0, tiled=True)  54.5 us
    another operation x6, other arithmetic, local(): factor_local = jnp.linalg.cholesky(diag_block)  24.8 us
    all_gather x2, blocking collectives, spread(): return jnp.sum(lax.all_gather(kept, axis), axis=0)  20.7 us
    another operation x4, other arithmetic, local(): jax.scipy.linalg.solve_triangular(lower_fac, matrix[:, first_col:first_co...  19.6 us
    all_to_all x1, waiting for transfers between devices, local(): lax.all_to_all(own_dense, 'link', split_axis=1, concat_axis=0, tiled=True)  19.3 us
    all_to_all x1, starting transfers between devices, local(): lax.all_to_all(own_dense, 'link', split_axis=1, concat_axis=0, tiled=True)  13 us
  transfers between devices with their start and end apart: 6, of which 6 were waited for; matrix products, arithmetic and copies ran while one was open for 0% of the time, Pallas kernels for 0%

profile of v1, /device:TPU:1, one launch (start us, length us, event | category | flops | bytes accessed | tf_op | source)
XLA Modules:
  0.0 513.7 jit_solution(5185980086118882535)
XLA Ops:
  6.5 0.0 copy-start
  6.5 0.0 copy-start.3
  6.5 0.0 all-gather.10.cloned.1.call-start
  6.5 0.7 multiply_sqrt_fusion
  7.2 1.4 convolution_convert_fusion
  8.6 0.3 copy.31
  9.0 0.7 constant_dynamic-slice_fusion
  9.7 0.0 all-gather.10.cloned.1.call-update
  9.7 0.2 all_to_all.14
  9.9 1.1 copy.19
  11.0 13.0 %all-to-all-start = ((bf16[16,64,256]{2,0,1:T(8,128)(2,1)}), bf16[16,64,256]{2,0,1:T(8,128)(2,1)S(1)}, u32[]{:S(2)}, u32[]{:S(2)}) async-start(bf16[16,64,256]{2,0,1:T(8,128)(2,1)} %copy.19), calls=%async_computation | async-start | bytes 1048576 | tf_op jit(solution)/shard_map/all_to_all | solution.py:42
  23.9 0.0 all-gather.16.cloned.1.call-start
  24.0 0.0 copy-done
  24.0 0.0 copy-done.3
  24.0 0.2 convolution_bitcast_fusion
  24.3 0.1 dynamic_slice.13
  24.4 19.3 %all-to-all-done = bf16[16,64,256]{2,0,1:T(8,128)(2,1)S(1)} async-done(((bf16[16,64,256]{2,0,1:T(8,128)(2,1)}), bf16[16,64,256]{2,0,1:T(8,128)(2,1)S(1)}, u32[]{:S(2)}, u32[]{:S(2)}) %all-to-all-start) | async-done | bytes 524320 | tf_op jit(solution)/shard_map/all_to_all | solution.py:42
  43.6 54.5 %all-gather.10.cloned.1.call-done = bf16[1024,4096]{1,0:T(8,128)(2,1)} async-done(((bf16[16,4096]{1,0:T(8,128)(2,1)}), bf16[1024,4096]{1,0:T(8,128)(2,1)}) %all-gather.10.cloned.1.call-update) | async-done | bytes 8388624 | tf_op jit(solution)/shard_map/all_gather | solution.py:44
  98.2 6.6 %convolution_add_fusion = f32[256,4096]{0,1:T(8,128)S(1)} fusion(bf16[1024,256]{1,0:T(8,128)(2,1)S(1)} %bitcast.72, bf16[1024,4096]{1,0:T(8,128)(2,1)} %all-gather.10.cloned.1.call-done, f32[256]{0:T(256)S(1)} %dynamic_slice.13, s32[256]{0:T(256)S(1)} %iota_add_fusion.1, s32[4096]{0:T(1024)S(1)} %iota_add_fusion), kind=kOutput, calls=%fused_computation.4 | convolution fusion | flops 2150629376 | bytes 13125632 | tf_op jit(solution)/shard_map/dot_general | solution.py:22
  104.8 0.0 copy-start.2
  104.8 2.0 copy-done.2
  106.8 0.1 copy.21
  106.9 0.9 fusion.14
  107.8 11.7 %cholesky.44 = f32[128,128]{1,0:T(8,128)S(1)} custom-call(f32[128,128]{1,0:T(8,128)S(1)} %fusion.14), custom_call_target="Cholesky" | custom-call | tf_op jit(solution)/shard_map/jit(cholesky)/cholesky | solution.py:59
  119.5 0.6 compare_reduce_fusion.1
  120.2 1.2 select_select_fusion.1
  121.4 0.0 all-gather.16.cloned.1.call-update
  121.4 0.0 all-gather.12.cloned.1.call-start
  121.5 75.9 %all-gather.16.cloned.1.call-done = f32[8192,128]{1,0:T(8,128)} async-done(((f32[128,128]{1,0:T(8,128)}), f32[8192,128]{1,0:T(8,128)}) %all-gather.16.cloned.1.call-update) | async-done | bytes 4194320 | tf_op jit(solution)/shard_map/all_gather | solution.py:11
  197.3 2.4 reduce_sum.42
  199.8 0.3 fusion.8
  200.1 9.8 %custom-call.6 = f32[1,128,128]{1,2,0:T(8,128)S(1)} custom-call(f32[1,128,128]{2,1,0:T(8,128)S(1)} %select_bitcast_fusion.1), custom_call_target="InvertDiagBlocksLowerTriangular" | custom-call | tf_op jit(solution)/shard_map/jit(_solve_triangular)/triangular_solve | solution.py:61
  209.9 1.2 convert_select_fusion.1
  211.1 10.3 %all-gather.1 = bf16[1024,128]{0,1:T(8,128)(2,1)S(1)} all-gather(bf16[256,128]{0,1:T(8,128)(2,1)S(1)} %get-tuple-element.6), channel_id=3, replica_groups=mesh['link'=64,'col'=4] {'col'}, dimensions={0}, use_global_device_ids=true | all-gather | bytes 327680 | tf_op jit(solution)/shard_map/all_gather | solution.py:11
  221.5 0.2 reshape.57
  221.6 1.0 reduce_sum.43
  222.6 0.0 all-gather.12.cloned.1.call-update
  222.6 0.2 all-gather.18.cloned.1.call-start
  222.8 75.1 %all-gather.12.cloned.1.call-done = bf16[16384,128]{0,1:T(8,128)(2,1)} async-done(((bf16[256,128]{0,1:T(8,128)(2,1)}), bf16[16384,128]{0,1:T(8,128)(2,1)}) %all-gather.12.cloned.1.call-update) | async-done | bytes 4194320 | tf_op jit(solution)/shard_map/all_gather | solution.py:72
  297.9 3.3 convolution_subtract_fusion.1
  301.2 0.0 copy-start.1
  301.2 2.0 copy-done.1
  303.3 0.1 copy.23
  303.3 0.9 fusion.12
  304.2 11.7 %cholesky.55 = f32[128,128]{1,0:T(8,128)S(1)} custom-call(f32[128,128]{1,0:T(8,128)S(1)} %fusion.12), custom_call_target="Cholesky" | custom-call | tf_op jit(solution)/shard_map/jit(cholesky)/cholesky | solution.py:59
  316.0 0.6 compare_reduce_fusion
  316.6 1.2 select_select_fusion
  317.8 0.0 all-gather.18.cloned.1.call-update
  317.8 0.0 all-gather.14.cloned.1.call-start
  317.9 78.5 %all-gather.18.cloned.1.call-done = f32[8192,128]{1,0:T(8,128)} async-done(((f32[128,128]{1,0:T(8,128)}), f32[8192,128]{1,0:T(8,128)}) %all-gather.18.cloned.1.call-update) | async-done | bytes 4194320 | tf_op jit(solution)/shard_map/all_gather | solution.py:11
  396.4 2.4 reduce_sum.44
  398.8 0.3 fusion.9
  399.2 9.8 %custom-call.7 = f32[1,128,128]{1,2,0:T(8,128)S(1)} custom-call(f32[1,128,128]{2,1,0:T(8,128)S(1)} %select_bitcast_fusion), custom_call_target="InvertDiagBlocksLowerTriangular" | custom-call | tf_op jit(solution)/shard_map/jit(_solve_triangular)/triangular_solve | solution.py:61
  409.0 1.2 convert_select_fusion
  410.2 10.3 %all-gather.3 = bf16[1024,128]{0,1:T(8,128)(2,1)S(1)} all-gather(bf16[256,128]{0,1:T(8,128)(2,1)S(1)} %get-tuple-element.9), channel_id=5, replica_groups=mesh['link'=64,'col'=4] {'col'}, dimensions={0}, use_global_device_ids=true | all-gather | bytes 327680 | tf_op jit(solution)/shard_map/all_gather | solution.py:11
  420.5 0.2 reshape.59
  420.7 1.0 reduce_sum.45
  421.7 0.0 all-gather.14.cloned.1.call-update
  421.7 75.3 %all-gather.14.cloned.1.call-done = bf16[16384,128]{0,1:T(8,128)(2,1)} async-done(((bf16[256,128]{0,1:T(8,128)(2,1)}), bf16[16384,128]{0,1:T(8,128)(2,1)}) %all-gather.14.cloned.1.call-update) | async-done | bytes 4194320 | tf_op jit(solution)/shard_map/all_gather | solution.py:72
  497.0 4.5 fusion.1
  501.6 5.6 %copy.25 = f32[256,4096]{1,0:T(8,128)} copy(f32[256,4096]{0,1:T(8,128)} %fusion.1) | data formatting | bytes 8388608 | tf_op jit(solution)/shard_map/jit(_where)/select_n | solution.py:80
  (12 shorter events, 0.1 us)
Async XLA Ops:
  6.5 17.5 %copy-start = (f32[16384]{0:T(1024)S(1)}, f32[16384]{0:T(1024)}, u32[]{:S(2)}) copy-start(f32[16384]{0:T(1024)} %param.11) | copy-start | bytes 196612
  6.5 17.5 %copy-start.3 = (s32[128]{0:T(128)S(1)}, s32[128]{0:T(128)}, u32[]{:S(2)}) copy-start(s32[128]{0:T(128)} %param.12) | copy-start | bytes 1540
  6.5 91.6 %all-gather.10.cloned.1.call-start = ((), (), s32[]{:S(2)}) async-start(), calls=%async_computation.1 | async-start | bytes 8519680 | tf_op jit(solution)/shard_map/all_gather | solution.py:44
  11.0 32.7 %all-to-all-start = ((bf16[16,64,256]{2,0,1:T(8,128)(2,1)}), bf16[16,64,256]{2,0,1:T(8,128)(2,1)S(1)}, u32[]{:S(2)}, u32[]{:S(2)}) async-start(bf16[16,64,256]{2,0,1:T(8,128)(2,1)} %copy.19), calls=%async_computation | async-start | bytes 1048576 | tf_op jit(solution)/shard_map/all_to_all | solution.py:42
  23.9 173.4 %all-gather.16.cloned.1.call-start = ((), (), s32[]{:S(2)}) async-start(), calls=%async_computation.4 | async-start | bytes 4259840 | tf_op jit(solution)/shard_map/all_gather | solution.py:11
  104.8 2.0 copy-start.2
  121.4 176.5 %all-gather.12.cloned.1.call-start = ((), (), s32[]{:S(2)}) async-start(), calls=%async_computation.2 | async-start | bytes 4259840 | tf_op jit(solution)/shard_map/all_gather | solution.py:72
  222.6 173.8 %all-gather.18.cloned.1.call-start = ((), (), s32[]{:S(2)}) async-start(), calls=%async_computation.5 | async-start | bytes 4259840 | tf_op jit(solution)/shard_map/all_gather | solution.py:11
  301.2 2.0 copy-start.1
  317.8 179.2 %all-gather.14.cloned.1.call-start = ((), (), s32[]{:S(2)}) async-start(), calls=%async_computation.3 | async-start | bytes 4259840 | tf_op jit(solution)/shard_map/all_gather | solution.py:72
Sparse Core Ops, SparseCore 0:
  10.1 88.0 all-gather.9
  121.5 75.7 all-gather.15
  222.7 75.1 all-gather.11
  317.9 78.4 all-gather.17
  421.8 75.1 all-gather.13
